TPU v7x, 128 devices: a whole 4x4x4 slice. The times are simulated.
128 devices in a mesh: req: 16 (over z, y), tensor: 8 (over x, core).
Axes of the slice: x: 4, y: 4, z: 4, core: 2. Of those that a mesh axis runs over, the one named last changes fastest.
Arguments:
- residual_input: bfloat16 [8192, 7168], P('req', 'tensor'), may hold values from -6 to 6
- input_norm_gain: float32 [7168], replicated, may hold values from 0.25 to 1.75
- query_weight: bfloat16 [7168, 4096], P(None, 'tensor'), may hold values from -0.09375 to 0.09375
- key_value_weight: bfloat16 [7168, 2048], P(None, 'tensor'), may hold values from -0.09375 to 0.09375
- output_weight: bfloat16 [4096, 7168], P('tensor'), may hold values from -0.375 to 0.375
- adapter_down_maps: bfloat16 [64, 48, 7168], P('req', None, 'tensor'), may hold values from -0.0625 to 0.0625
- adapter_query_up: bfloat16 [64, 16, 4096], P('req', None, 'tensor'), may hold values from -0.375 to 0.375
- adapter_key_value_up: bfloat16 [64, 2, 16, 1024], P('req', None, None, 'tensor'), may hold values from -0.375 to 0.375
- adapter_output_down: bfloat16 [64, 16, 4096], P('req', None, 'tensor'), may hold values from -0.375 to 0.375
- adapter_output_up: bfloat16 [64, 16, 7168], P('req', None, 'tensor'), may hold values from -0.375 to 0.375
- request_adapter: int32 [64], P('req'), may hold values from 0 to 63
- prompt_length: int32 [64], P('req'), may hold values from 32 to 128, as said below
- cache_length: int32 [32], replicated, may hold values from 16 to 2048, as said below
- first_page_device: int32 [32], replicated, may hold values from 0 to 15
- page_slot_table: int32 [16, 32], P('req'), may hold values from 0 to 31, as said below
- cache_page_pool: bfloat16 [512, 128, 2048], P('req', None, 'tensor'), may hold values from -200 to 200
Outputs:
- block_out: bfloat16 [8192, 7168], P('req', 'tensor')
Inputs may be any that keep to these rules, and one draw needn't show every extreme that they name: `prompt_length`: some request in every draw fills all 128 rows of its block. `cache_length`: some cache in every draw has 2048 positions. `page_slot_table`: each row is a permutation of the cached requests over the pool slots of one device.
All inputs are finite; a program needn't handle non-finite values.
Results may differ from a plain program's by a relative error of at most 0.035.
Values may be sent and summed in bfloat16 or wider, within the bound.
No kernel may reach another device: no remote copies, remote signals or barrier semaphores. Data moves between devices by JAX's collectives and lax.ppermute only.
A program may use at most 128 MiB of HBM per device.

v0:
```python
import jax
import jax.numpy as jnp
from jax import lax
from jax.sharding import PartitionSpec as P

HEAD_SIZE = 128
ROPE_BASE = 5000000.0
ADAPTER_SCALE = 2.0
EPSILON = 1e-05
NEG_FILL = -1e30


def rotate(vectors, positions):
    half_dim = vectors.shape[-1] // 2
    frequency = ROPE_BASE ** (-jnp.arange(half_dim, dtype=jnp.float32) / half_dim)
    angles = positions.astype(jnp.float32)[..., None] * frequency
    cosine = jnp.cos(angles)
    sine_part = jnp.sin(angles)
    front_half = vectors[..., :half_dim]
    back_half = vectors[..., half_dim:]
    return jnp.concatenate(
        [front_half * cosine - back_half * sine_part, back_half * cosine + front_half * sine_part],
        axis=-1,
    )


def partial_softmax(query_rows, key_rows, value_rows, allowed):
    score_scale = query_rows.shape[-1] ** (-0.5)
    scores = (
        jnp.einsum("bsvgd,bkvd->bvsgk", query_rows, key_rows, preferred_element_type=jnp.float32)
        * score_scale
    )
    spread_mask = allowed[:, None, :, None, :]
    scores = jnp.where(spread_mask, scores, NEG_FILL)
    peak_scores = jnp.max(scores, axis=-1)
    weights = jnp.where(spread_mask, jnp.exp(scores - peak_scores[..., None]), 0.0)
    totals = jnp.sum(weights, axis=-1)
    summed = jnp.einsum(
        "bvsgk,bkvd->bvsgd",
        weights.astype(jnp.bfloat16),
        value_rows,
        preferred_element_type=jnp.float32,
    )
    return (peak_scores, totals, summed)


def local(
    residual_input,
    input_norm_gain,
    query_weight,
    key_value_weight,
    output_weight,
    adapter_down_maps,
    adapter_query_up,
    adapter_key_value_up,
    adapter_output_down,
    adapter_output_up,
    request_adapter,
    prompt_length,
    cache_length,
    first_page_device,
    page_slot_table,
    cache_page_pool,
):
    holders = lax.axis_size("req")
    req_index = lax.axis_index("req")
    tensor_index = lax.axis_index("tensor")
    request_number = request_adapter.shape[0]
    cached_count = request_number // 2
    row_count = residual_input.shape[0]
    request_slot_rows = row_count // request_number
    piece_width = residual_input.shape[1]
    local_kv = key_value_weight.shape[1] // (2 * HEAD_SIZE)
    group_size = query_weight.shape[1] // (HEAD_SIZE * local_kv)
    page_rows = cache_page_pool.shape[1]
    gathered = lax.all_gather(residual_input, "tensor", axis=1, tiled=True)
    widened = gathered.astype(jnp.float32)
    inverse = lax.rsqrt(jnp.mean(widened * widened, axis=1, keepdims=True) + EPSILON)
    normed = (widened * inverse * input_norm_gain).astype(jnp.bfloat16)
    empty_sel = tuple(
        (
            jnp.zeros((request_number,) + adapter_lookup.shape[1:], jnp.bfloat16)
            for adapter_lookup in (
                adapter_down_maps,
                adapter_query_up,
                adapter_key_value_up,
                adapter_output_down,
                adapter_output_up,
            )
        )
    )
    pieces = (
        lax.all_gather(adapter_down_maps, "req", axis=0, tiled=True),
        lax.all_gather(adapter_query_up, "req", axis=0, tiled=True),
        lax.all_gather(adapter_key_value_up, "req", axis=0, tiled=True),
        lax.all_gather(adapter_output_down, "req", axis=0, tiled=True),
        lax.all_gather(adapter_output_up, "req", axis=0, tiled=True),
    )
    block_count = pieces[0].shape[0]
    adapter_ids = jnp.arange(block_count, dtype=jnp.int32)
    onehot = (request_adapter[:, None] == adapter_ids[None, :]).astype(jnp.bfloat16)
    down_picked, query_picked, key_value_picked, output_down_picked, oup_sel = tuple(
        (
            jnp.dot(onehot, segment.reshape(block_count, -1), preferred_element_type=jnp.float32)
            .reshape(held_sel.shape)
            .astype(jnp.bfloat16)
            for held_sel, segment in zip(empty_sel, pieces)
        )
    )
    adapter_rank_size = query_picked.shape[1]
    own_columns = lax.dynamic_slice_in_dim(
        normed, tensor_index * piece_width, piece_width, 1
    ).reshape(request_number, request_slot_rows, piece_width)
    partial_low = jnp.einsum(
        "rsd,rkd->rsk", own_columns, down_picked, preferred_element_type=jnp.float32
    )
    reduced_input = (
        lax.psum(partial_low.reshape(-1, 128).astype(jnp.bfloat16), "tensor")
        .astype(jnp.float32)
        .reshape(request_number, request_slot_rows, 3 * adapter_rank_size)
        .astype(jnp.bfloat16)
    )
    query_rows = jnp.dot(normed, query_weight, preferred_element_type=jnp.float32).reshape(
        request_number, request_slot_rows, -1
    )
    query_rows = query_rows + ADAPTER_SCALE * jnp.einsum(
        "ibm,imf->ibf",
        reduced_input[..., :adapter_rank_size],
        query_picked,
        preferred_element_type=jnp.float32,
    )
    keyval = jnp.dot(normed, key_value_weight, preferred_element_type=jnp.float32).reshape(
        request_number, request_slot_rows, local_kv, 2 * HEAD_SIZE
    )
    key_add = jnp.einsum(
        "ibm,imf->ibf",
        reduced_input[..., adapter_rank_size : 2 * adapter_rank_size],
        key_value_picked[:, 0],
        preferred_element_type=jnp.float32,
    ).reshape(request_number, request_slot_rows, local_kv, HEAD_SIZE)
    value_add = jnp.einsum(
        "ibm,imf->ibf",
        reduced_input[..., 2 * adapter_rank_size :],
        key_value_picked[:, 1],
        preferred_element_type=jnp.float32,
    ).reshape(request_number, request_slot_rows, local_kv, HEAD_SIZE)
    my_cache = lax.dynamic_slice_in_dim(cache_length, req_index * cached_count, cached_count, 0)
    offsets = jnp.stack([jnp.zeros_like(my_cache), my_cache], axis=1).reshape(request_number)
    slot_index = jnp.arange(request_slot_rows, dtype=jnp.int32)
    positions = offsets[:, None] + slot_index[None, :]
    query_rot = rotate(
        query_rows.reshape(request_number, request_slot_rows, local_kv, group_size, HEAD_SIZE),
        positions[:, :, None, None],
    ).astype(jnp.bfloat16)
    key_rot = rotate(keyval[..., :HEAD_SIZE] + key_add, positions[:, :, None]).astype(jnp.bfloat16)
    value_new = (keyval[..., HEAD_SIZE:] + value_add).astype(jnp.bfloat16)
    causal = slot_index[None, :, None] >= slot_index[None, None, :]
    own_mask = causal & (slot_index[None, None, :] < prompt_length[:, None, None])
    own_part = partial_softmax(query_rot, key_rot, value_new, own_mask)
    asked_queries = query_rot[1::2]
    slot_order = page_slot_table[0].reshape(holders, cached_count).T.reshape(-1)
    outgoing = cache_page_pool[slot_order].reshape(
        cached_count, holders, page_rows, cache_page_pool.shape[2]
    )
    arrived = lax.all_to_all(outgoing, "req", split_axis=1, concat_axis=1, tiled=True)
    my_base = lax.dynamic_slice_in_dim(first_page_device, req_index * cached_count, cached_count, 0)
    page_of = (jnp.arange(holders, dtype=jnp.int32)[None, :] - my_base[:, None]) % holders
    key_pos = (
        page_of[:, :, None] * page_rows + jnp.arange(page_rows, dtype=jnp.int32)[None, None, :]
    ).reshape(cached_count, holders * page_rows)
    entries = arrived.reshape(cached_count, holders * page_rows, local_kv, 2 * HEAD_SIZE)
    visible = jnp.broadcast_to(
        (key_pos < my_cache[:, None])[:, None, :],
        (cached_count, request_slot_rows, holders * page_rows),
    )
    cache_part = partial_softmax(
        asked_queries, entries[..., :HEAD_SIZE], entries[..., HEAD_SIZE:], visible
    )
    filler = jnp.full_like(cache_part[0], NEG_FILL)
    spread_peak = jnp.stack([filler, cache_part[0]], axis=1).reshape(own_part[0].shape)
    spread_total = jnp.stack([jnp.zeros_like(cache_part[1]), cache_part[1]], axis=1).reshape(
        own_part[1].shape
    )
    spread_sum = jnp.stack([jnp.zeros_like(cache_part[2]), cache_part[2]], axis=1).reshape(
        own_part[2].shape
    )
    highest_all = jnp.maximum(own_part[0], spread_peak)
    own_weight = jnp.exp(own_part[0] - highest_all)
    cache_weight = jnp.exp(spread_peak - highest_all)
    denominator = own_part[1] * own_weight + spread_total * cache_weight
    numerator = own_part[2] * own_weight[..., None] + spread_sum * cache_weight[..., None]
    live_rows = slot_index[None, :] < prompt_length[:, None]
    attended = jnp.where(
        live_rows[:, None, :, None, None], numerator / denominator[..., None], 0.0
    ).astype(jnp.bfloat16)
    attended = jnp.transpose(attended, (0, 2, 1, 3, 4)).reshape(row_count, -1)
    head_terms = jnp.dot(attended, output_weight, preferred_element_type=jnp.float32)
    low_part = jnp.einsum(
        "rsc,rkc->rsk",
        attended.reshape(request_number, request_slot_rows, -1),
        output_down_picked,
        preferred_element_type=jnp.float32,
    )
    reduced_output = (
        lax.psum(low_part.reshape(-1, 128).astype(jnp.bfloat16), "tensor")
        .astype(jnp.float32)
        .reshape(request_number, request_slot_rows, adapter_rank_size)
        .astype(jnp.bfloat16)
    )
    head_total = lax.psum_scatter(
        head_terms.astype(jnp.bfloat16), "tensor", scatter_dimension=1, tiled=True
    ).astype(jnp.float32)
    adapter_output = jnp.einsum(
        "ibm,imf->ibf", reduced_output, oup_sel, preferred_element_type=jnp.float32
    ).reshape(row_count, -1)
    return (head_total + ADAPTER_SCALE * adapter_output).astype(jnp.bfloat16)


def solution(mesh):
    placed = (
        P("req", "tensor"),
        P(),
        P(None, "tensor"),
        P(None, "tensor"),
        P("tensor", None),
        P("req", None, "tensor"),
        P("req", None, "tensor"),
        P("req", None, None, "tensor"),
        P("req", None, "tensor"),
        P("req", None, "tensor"),
        P("req"),
        P("req"),
        P(),
        P(),
        P("req", None),
        P("req", None, "tensor"),
    )
    return jax.shard_map(
        local, mesh=mesh, in_specs=placed, out_specs=P("req", "tensor"), check_vma=False
    )
```

profile of v0, /device:TPU:1, one launch (start us, length us, event | category | flops | bytes accessed | tf_op | source)
XLA Modules:
  0.0 329.6 jit_solution(5925808227693249332)
XLA Ops:
  6.5 0.7 all-gather.10.cloned.1.call-update
  7.3 0.7 all-gather.8.cloned.1.call-update
  8.1 0.7 all-gather.6.cloned.1.call-update
  8.8 0.5 all-gather.12.cloned.1.call-update
  9.3 0.5 broadcast.279
  9.9 1.3 reduce.11
  11.3 0.1 copy.80
  11.3 0.1 reshape.501
  11.5 2.0 gather_fusion
  13.5 3.1 copy.81
  16.6 8.6 %all-to-all-start = ((bf16[2,16,128,256]{3,2,0,1:T(8,128)(2,1)}), bf16[2,16,128,256]{3,2,0,1:T(8,128)(2,1)S(1)}, u32[]{:S(2)}, u32[]{:S(2)}) async-start(bf16[2,16,128,256]{3,2,0,1:T(8,128)(2,1)} %copy.81), calls=%async_computation | async-start | bytes 4194304 | tf_op jit(solution)/shard_map/all_to_all | solution.py:165
  25.2 0.5 all-gather.14.cloned.1.call-update
  25.9 0.1 copy.110
  26.1 0.1 add.134
  26.3 43.4 %all_gather.21 = bf16[64,2,16,128]{3,2,1,0:T(8,128)(2,1)S(1)} all-gather(bf16[4,2,16,128]{3,2,1,0:T(8,128)(2,1)S(1)} %copy-done.7), channel_id=1, replica_groups=mesh['req'=16,'tensor'=8] {'req'}, dimensions={0}, use_global_device_ids=true | all-gather | bytes 557056 | tf_op jit(solution)/shard_map/all_gather | solution.py:95
  70.0 0.2 copy.182
  70.3 0.1 copy.120
  70.4 0.3 convolution_convert_fusion.4
  70.7 0.6 slice_bitcast_fusion.4
  71.3 0.1 broadcast_and_fusion
  71.5 1.8 multiply_cosine_fusion
  73.3 2.4 convolution_convert_fusion.2
  75.8 1.5 copy.82
  77.3 54.5 %all-gather.8.cloned.1.call-done = bf16[64,48,896]{2,1,0:T(8,128)(2,1)} async-done(((bf16[4,48,896]{2,1,0:T(8,128)(2,1)}), bf16[64,48,896]{2,1,0:T(8,128)(2,1)}) %all-gather.8.cloned.1.call-update) | async-done | bytes 5505040 | tf_op jit(solution)/shard_map/all_gather | solution.py:93
  131.8 3.8 %fusion.25 = bf16[4,48,896]{2,0,1:T(4,128)(2,1)S(1)} fusion(s32[4]{0:T(128)S(1)} %copy-done.11, bf16[8,8,48,896]{3,2,1,0:T(8,128)(2,1)} %bitcast.206), kind=kOutput, calls=%fused_computation.33 | convolution fusion | flops 22192384 | bytes 5849104 | tf_op jit(solution)/shard_map/dot_general | solution.py:104
  135.6 43.3 %all-gather.6.cloned.1.call-done = bf16[512,7168]{1,0:T(8,128)(2,1)} async-done(((bf16[512,896]{1,0:T(8,128)(2,1)}), bf16[512,7168]{1,0:T(8,128)(2,1)}) %all-gather.6.cloned.1.call-update) | async-done | bytes 7340048 | tf_op jit(solution)/shard_map/all_gather | solution.py:76
  178.9 4.7 %fusion = f32[512]{0:T(512)S(1)} fusion(bf16[512,7168]{1,0:T(8,128)(2,1)} %all-gather.6.cloned.1.call-done), kind=kLoop, calls=%fused_computation.3 | loop fusion | flops 11009536 | bytes 7342080 | tf_op jit(solution)/shard_map/reduce_sum | solution.py:78
  183.6 0.4 copy-done.3
  184.0 5.8 %fusion.2 = bf16[512,7168]{1,0:T(8,128)(2,1)} fusion(bf16[512,7168]{1,0:T(8,128)(2,1)S(1)} %copy-done.3, f32[7168]{0:T(1024)S(1)} %copy-done.8, f32[512]{0:T(512)S(1)} %add_rsqrt_fusion), kind=kLoop, calls=%fused_computation.5 | loop fusion | flops 14680064 | bytes 14710784 | tf_op jit(solution)/shard_map/convert_element_type | solution.py:79
  189.8 1.3 constant_dynamic-slice_fusion
  191.1 0.5 convolution_convert_fusion.3
  191.5 21.7 %psum.14 = bf16[4,128,48]{1,2,0:T(8,128)(2,1)S(1)} all-reduce(bf16[4,128,48]{1,2,0:T(8,128)(2,1)S(1)} %convolution_convert_fusion.3), channel_id=1, replica_groups=mesh['req'=16,'tensor'=8] {'tensor'}, use_global_device_ids=true, to_apply=%region_1.0 | all-reduce | flops 24576 | bytes 98304 | tf_op jit(solution)/shard_map/psum | solution.py:118
  213.2 8.6 %fusion.102 = f32[512,512]{1,0:T(8,128)S(1)} fusion(bf16[512,7168]{1,0:T(8,128)(2,1)} %fusion.2, bf16[7168,512]{1,0:T(8,128)(2,1)} %param.18), kind=kOutput, calls=%fused_computation.141 | convolution fusion | flops 3758096384 | bytes 15728640 | tf_op jit(solution)/shard_map/dot_general | solution.py:123
  221.8 0.3 fusion.20
  222.1 0.4 reshape.494
  222.5 0.6 fusion.100
  223.1 6.3 %fusion.103 = f32[512,256]{1,0:T(8,128)S(1)} fusion(bf16[512,7168]{1,0:T(8,128)(2,1)} %fusion.2, bf16[7168,256]{1,0:T(8,128)(2,1)} %param.19), kind=kOutput, calls=%fused_computation.142 | convolution fusion | flops 1879048192 | bytes 11534336 | tf_op jit(solution)/shard_map/dot_general | solution.py:132
  229.5 0.3 subtract_convert_fusion
  229.8 0.3 pad_maximum_fusion
  230.1 1.5 fusion.3
  231.6 3.2 copy-done.2
  234.9 2.8 fusion.4
  237.6 0.7 slice.61
  238.4 1.1 copy.109
  239.4 0.7 stack.31
  240.1 4.6 %fusion.22 = f32[2,1,1,128,4,128]{3,5,4,1,0,2:T(8,128)S(1)} fusion(f32[2,128,4,2048]{3,1,2,0:T(8,128)} %copy-done.2, f32[2,128,4]{1,2,0:T(4,128)S(1)} %get-tuple-element.18, pred[2,2048]{1,0:T(4,128)(4,1)S(1)} %fusion.71, bf16[2,2048,1,256]{3,1,0,2:T(8,128)(2,1)S(1)} %bitcast.191), kind=kOutput, calls=%fused_computation.32 | convolution fusion | flops 547356672 | bytes 9973760 | tf_op jit(solution)/shard_map/bvsgk,bkvd->bvsgd/dot_general | solution.py:38
  244.8 0.2 fusion.28
  245.1 0.6 fusion.70
  245.7 0.5 fusion.101
  246.2 0.2 fusion.40
  246.4 1.1 bitcast_multiply_fusion
  247.5 1.9 fusion.21
  249.4 0.3 copy.86
  249.7 9.4 %convolution_convert_fusion = bf16[512,7168]{1,0:T(8,128)(2,1)} fusion(bf16[512,7168]{1,0:T(8,128)(2,1)} %param.20, bf16[64,8,4,128]{3,2,1,0:T(4,128)(2,1)S(1)} %bitcast.200), kind=kOutput, calls=%fused_computation.6 | convolution fusion | flops 3761766400 | bytes 15204352 | tf_op jit(solution)/shard_map/dot_general | solution.py:197
  259.2 10.5 %copy.105 = bf16[512,7168]{0,1:T(8,128)(2,1)} copy(bf16[512,7168]{1,0:T(8,128)(2,1)} %convolution_convert_fusion) | data formatting | bytes 14680064
  269.7 0.6 copy-done.12
  270.3 2.5 convolution_convert_fusion.1
  272.7 2.0 fusion.31
  274.7 0.2 convolution_convert_fusion.5
  274.9 24.3 %psum.15 = bf16[4,128,16]{1,2,0:T(8,128)(2,1)S(1)} all-reduce(bf16[4,128,16]{1,2,0:T(8,128)(2,1)S(1)} %convolution_convert_fusion.5), channel_id=1, replica_groups=mesh['req'=16,'tensor'=8] {'tensor'}, use_global_device_ids=true, to_apply=%region_7.8 | all-reduce | flops 8192 | bytes 32768 | tf_op jit(solution)/shard_map/psum | solution.py:205
  299.2 1.8 convolution_multiply_fusion
  300.9 17.8 %reduce-scatter.4.cloned.1.call-done = bf16[896,512]{1,0:T(8,128)(2,1)} async-done(((bf16[7168,512]{1,0:T(8,128)(2,1)}), bf16[896,512]{1,0:T(8,128)(2,1)}) %reduce-scatter.4.cloned.1.call-update) | async-done | bytes 917520
  318.7 1.5 copy.106
  320.2 2.6 fusion.15
  (61 shorter events, 1.3 us)
Async XLA Ops:
  6.5 4.9 %copy-start = (bf16[32,128,256]{2,1,0:T(8,128)(2,1)S(1)}, bf16[32,128,256]{2,1,0:T(8,128)(2,1)}, u32[]{:S(2)}) copy-start(bf16[32,128,256]{2,1,0:T(8,128)(2,1)} %param.31) | copy-start | bytes 6291460
  6.5 19.3 %copy-start.16 = (s32[32]{0:T(128)S(1)}, s32[32]{0:T(128)}, u32[]{:S(2)}) copy-start(s32[32]{0:T(128)} %param.28) | copy-start | bytes 388
  6.5 19.7 %copy-start.7 = (bf16[4,2,16,128]{3,2,1,0:T(8,128)(2,1)S(1)}, bf16[4,2,16,128]{3,2,1,0:T(8,128)(2,1)}, u32[]{:S(2)}) copy-start(bf16[4,2,16,128]{3,2,1,0:T(8,128)(2,1)} %param.23) | copy-start | bytes 98308
  6.5 66.8 %all-gather.10.cloned.1.call-start = ((), (), s32[]{:S(2)}) async-start(), calls=%async_computation.4 | async-start | bytes 1114112 | tf_op jit(solution)/shard_map/all_gather | solution.py:94
  7.3 62.4 %copy-start.14 = (s32[4]{0:T(128)S(1)}, s32[4]{0:T(128)}, u32[]{:S(2)}) copy-start(s32[4]{0:T(128)} %param.27) | copy-start | bytes 52
  7.3 62.5 %copy-start.15 = (s32[32]{0:T(128)S(1)}, s32[32]{0:T(128)}, u32[]{:S(2)}) copy-start(s32[32]{0:T(128)} %param.29) | copy-start | bytes 388
  7.3 124.5 %all-gather.8.cloned.1.call-start = ((), (), s32[]{:S(2)}) async-start(), calls=%async_computation.3 | async-start | bytes 5849088 | tf_op jit(solution)/shard_map/all_gather | solution.py:93
  8.0 170.8 %all-gather.6.cloned.1.call-start = ((), (), s32[]{:S(2)}) async-start(), calls=%async_computation.2 | async-start | bytes 8257536 | tf_op jit(solution)/shard_map/all_gather | solution.py:76
  8.8 260.9 %all-gather.12.cloned.1.call-start = ((), (), s32[]{:S(2)}) async-start(), calls=%async_computation.5 | async-start | bytes 1114112 | tf_op jit(solution)/shard_map/all_gather | solution.py:96
  11.5 59.0 %copy-start.11 = (s32[4]{0:T(128)S(1)}, s32[4]{0:T(128)}, u32[]{:S(2)}) copy-start(s32[4]{0:T(128)} %param.26) | copy-start | bytes 52
  16.6 59.2 %all-to-all-start = ((bf16[2,16,128,256]{3,2,0,1:T(8,128)(2,1)}), bf16[2,16,128,256]{3,2,0,1:T(8,128)(2,1)S(1)}, u32[]{:S(2)}, u32[]{:S(2)}) async-start(bf16[2,16,128,256]{3,2,0,1:T(8,128)(2,1)} %copy.81), calls=%async_computation | async-start | bytes 4194304 | tf_op jit(solution)/shard_map/all_to_all | solution.py:165
  25.2 247.6 %all-gather.14.cloned.1.call-start = ((), (), s32[]{:S(2)}) async-start(), calls=%async_computation.6 | async-start | bytes 1949696 | tf_op jit(solution)/shard_map/all_gather | solution.py:97
  25.8 292.9 %reduce-scatter.4.cloned.1.call-start = ((), (), s32[]{:S(2)}) async-start(), calls=%async_computation.7 | async-start | bytes 8257536
  69.8 65.8 %copy-start.13 = (pred[4,128]{1,0:T(4,128)(4,1)}, pred[4,128]{1,0:T(4,128)(4,1)S(1)}, u32[]{:S(2)}) copy-start(pred[4,128]{1,0:T(4,128)(4,1)S(1)} %iota_compare_fusion.2) | copy-start | bytes 1540
  70.0 65.6 %copy-start.9 = (f32[64]{0:T(128)}, f32[64]{0:T(128)S(1)}, u32[]{:S(2)}) copy-start(f32[64]{0:T(128)S(1)} %multiply_power_fusion) | copy-start | bytes 772
  131.8 51.8 %copy-start.8 = (f32[7168]{0:T(1024)S(1)}, f32[7168]{0:T(1024)}, u32[]{:S(2)}) copy-start(f32[7168]{0:T(1024)} %param.17) | copy-start | bytes 86020
  178.9 5.2 %copy-start.3 = (bf16[512,7168]{1,0:T(8,128)(2,1)S(1)}, bf16[512,7168]{1,0:T(8,128)(2,1)}, u32[]{:S(2)}) copy-start(bf16[512,7168]{1,0:T(8,128)(2,1)} %all-gather.6.cloned.1.call-done) | copy-start | bytes 22020100
  223.1 6.4 %copy-start.5 = (f32[4,128,64]{2,1,0:T(8,128)S(1)}, f32[4,128,64]{2,1,0:T(8,128)}, u32[]{:S(2)}) copy-start(f32[4,128,64]{2,1,0:T(8,128)} %get-tuple-element.17) | copy-start | bytes 393220
  223.1 7.0 %copy-start.4 = (bf16[2,16,128,256]{3,2,1,0:T(8,128)(2,1)S(1)}, bf16[2,16,128,256]{3,2,1,0:T(8,128)(2,1)}, u32[]{:S(2)}) copy-start(bf16[2,16,128,256]{3,2,1,0:T(8,128)(2,1)} %copy.82) | copy-start | bytes 6291460
  229.5 8.2 %copy-start.6 = (f32[512,256]{1,0:T(8,128)}, f32[512,256]{1,0:T(8,128)S(1)}, u32[]{:S(2)}) copy-start(f32[512,256]{1,0:T(8,128)S(1)} %fusion.103) | copy-start | bytes 1572868
  231.6 3.2 copy-start.2
  240.1 5.0 %copy-start.10 = (f32[64]{0:T(128)S(1)}, f32[64]{0:T(128)}, u32[]{:S(2)}) copy-start(f32[64]{0:T(128)} %copy-done.9) | copy-start | bytes 772
  269.6 0.7 copy-start.12
  269.6 53.2 %copy-start.1 = (bf16[32,128,256]{2,1,0:T(8,128)(2,1)S(1)}, bf16[32,128,256]{2,1,0:T(8,128)(2,1)}, u32[]{:S(2)}) copy-start(bf16[32,128,256]{2,1,0:T(8,128)(2,1)} %param.31) | copy-start | bytes 6291460
Sparse Core Ops, SparseCore 0:
  9.5 61.4 all-gather.9
  73.1 58.6 all-gather.7
  133.5 45.3 all-gather.5
  180.8 40.6 all-gather.11
  223.5 44.1 all-gather.13
  270.0 48.6 reduce-scatter.3
where the time goes:
time: 330 us
  waiting for transfers between devices  119 us (36%)
  blocking collectives  89.4 us (27%)
  matrix products  46.7 us (14%)
  local copies, waits for them, and re-layouts  30.3 us (9%)
  other arithmetic  22 us (7%)
  between operations  13.8 us (4%)
  starting transfers between devices  8.78 us (3%)
    all_gather x1, waiting for transfers between devices, local(): lax.all_gather(adapter_down_maps, 'req', axis=0, tiled=True)  54.5 us
    all_gather x1, blocking collectives, local(): lax.all_gather(adapter_key_value_up, 'req', axis=0, tiled=True)  43.4 us
    all_gather x1, waiting for transfers between devices, local(): gathered = lax.all_gather(residual_input, 'tensor', axis=1, tiled=True)  43.3 us
    psum x1, blocking collectives, local(): lax.psum(low_part.reshape(-1, 128).astype(jnp.bfloat16), 'tensor')  24.3 us
    psum x1, blocking collectives, local(): lax.psum(partial_low.reshape(-1, 128).astype(jnp.bfloat16), 'tensor')  21.7 us
    unnamed x7, waiting for transfers between devices  20.9 us
    unnamed x42, local copies, waits for them, and re-layouts  18.3 us
    dot_general x5, matrix products, local(): jnp.dot(onehot, segment.reshape(block_count, -1), preferred_element_type=...  10.9 us
  transfers between devices with their start and end apart: 7, of which 3 were waited for; matrix products, arithmetic and copies ran while one was open for 27% of the time, Pallas kernels for 0%

commit v1 on v0

--- a/solution.py
+++ b/solution.py
@@ -73,7 +73,33 @@
     local_kv = key_value_weight.shape[1] // (2 * HEAD_SIZE)
     group_size = query_weight.shape[1] // (HEAD_SIZE * local_kv)
     page_rows = cache_page_pool.shape[1]
-    gathered = lax.all_gather(residual_input, "tensor", axis=1, tiled=True)
+
+    def set_packet_all(row_data):
+        in_order = []
+        after, met_up, high = (lax.axis_size("tensor"), lax.axis_index("tensor"), row_data.shape[1])
+        for dev_i, kk in enumerate(row_data.shape):
+            in_order.append(kk * after if dev_i == 1 else kk)
+        even = kept_arr = row_data
+        r2 = lax.dynamic_update_slice_in_dim(
+            jnp.zeros(in_order, row_data.dtype), row_data, met_up * high, axis=1
+        )
+        for no in [*range(1, after // 2 + 1)]:
+            buffers = []
+            for dev_i in [*range(after)]:
+                buffers.append((dev_i, (dev_i + 1) % after))
+            even = lax.ppermute(even, "tensor", buffers)
+            r2 = lax.dynamic_update_slice_in_dim(r2, even, (met_up - no) % after * high, axis=1)
+            if 2 * no < after:
+                chunks = []
+                for dev_i in tuple(range(after)):
+                    chunks.append((dev_i, (dev_i - 1) % after))
+                kept_arr = lax.ppermute(kept_arr, "tensor", chunks)
+                r2 = lax.dynamic_update_slice_in_dim(
+                    r2, kept_arr, (met_up + no) % after * high, axis=1
+                )
+        return r2
+
+    gathered = set_packet_all(residual_input)
     widened = gathered.astype(jnp.float32)
     inverse = lax.rsqrt(jnp.mean(widened * widened, axis=1, keepdims=True) + EPSILON)
     normed = (widened * inverse * input_norm_gain).astype(jnp.bfloat16)

time: 330 us -> 282 us (0.85)
  waiting for transfers between devices: 119 us -> 40.8 us
  local copies, waits for them, and re-layouts: 30.3 us -> 44.3 us
  starting transfers between devices: 8.78 us -> 22.7 us
    all_gather x1, waiting for transfers between devices: 54.5 us -> 0.01 us  [local(): lax.all_gather(adapter_down_maps, 'req', axis=0, tiled=True)]
    all_gather x1 -> x0, waiting for transfers between devices: 43.3 us -> none  [local(): gathered = lax.all_gather(residual_input, 'tensor', axis=1, tiled=True)]
    dynamic_update_slice x0 -> x8, local copies, waits for them, and re-layouts: none -> 15.6 us  [the longest x4 7.82 us: set_packet_all(): lax.dynamic_update_slice_in_dim(r2, even, (met_up - no) % after * high, a...]
    ppermute x0 -> x7, starting transfers between devices: none -> 14.6 us  [the longest x4 14.6 us: set_packet_all(): even = lax.ppermute(even, 'tensor', buffers)]
    ppermute x0 -> x7, waiting for transfers between devices: none -> 9.49 us  [the longest x4 9.41 us: set_packet_all(): even = lax.ppermute(even, 'tensor', buffers)]
    all_gather x1, waiting for transfers between devices: 0.01 us -> 5.49 us  [local(): lax.all_gather(adapter_output_up, 'req', axis=0, tiled=True)]
    unnamed x7 -> x6, waiting for transfers between devices: 20.9 us -> 25.8 us
    unnamed x42 -> x38, local copies, waits for them, and re-layouts: 18.3 us -> 14.3 us
  transfers between devices with their start and end apart: 7 -> 13, of which waited for: 3 -> 5; matrix products, arithmetic and copies ran while one was open for 27% -> 40% of each run, Pallas kernels for 0% -> 0%
where the time goes in v1:
time: 282 us; the launch traced here: 281 us
  blocking collectives  88.2 us (31%)
  matrix products  47.6 us (17%)
  local copies, waits for them, and re-layouts  44.3 us (16%)
  waiting for transfers between devices  40.8 us (14%)
  other arithmetic  24 us (9%)
  starting transfers between devices  22.7 us (8%)
  between operations  13.5 us (5%)
    all_gather x1, blocking collectives, local(): lax.all_gather(adapter_key_value_up, 'req', axis=0, tiled=True)  41.9 us
    unnamed x6, waiting for transfers between devices  25.8 us
    psum x1, blocking collectives, local(): lax.psum(partial_low.reshape(-1, 128).astype(jnp.bfloat16), 'tensor')  23.4 us
    psum x1, blocking collectives, local(): lax.psum(low_part.reshape(-1, 128).astype(jnp.bfloat16), 'tensor')  22.9 us
    ppermute x4, starting transfers between devices, set_packet_all(): even = lax.ppermute(even, 'tensor', buffers)  14.6 us
    unnamed x38, local copies, waits for them, and re-layouts  14.3 us
    dot_general x5, matrix products, local(): jnp.dot(onehot, segment.reshape(block_count, -1), preferred_element_type=...  11 us
    dot_general x1, matrix products, local(): jnp.dot(normed, query_weight, preferred_element_type=jnp.float32)  10.3 us
  transfers between devices with their start and end apart: 13, of which 5 were waited for; matrix products, arithmetic and copies ran while one was open for 40% of the time, Pallas kernels for 0%

profile of v1, /device:TPU:1, one launch (start us, length us, event | category | flops | bytes accessed | tf_op | source)
XLA Modules:
  0.0 281.2 jit_solution(17909278081929096319)
XLA Ops:
  6.5 0.7 all-gather.7.cloned.1.call-update
  7.3 0.7 all-gather.5.cloned.1.call-update
  8.1 0.7 all-gather.9.cloned.1.call-update
  8.7 2.6 collective-permute-start
  11.3 0.5 broadcast.286
  11.9 1.3 reduce.11
  13.5 2.0 gather_fusion
  15.5 3.1 %copy.81 = bf16[2,16,128,256]{3,2,0,1:T(8,128)(2,1)} copy(bf16[2,16,128,256]{3,2,1,0:T(8,128)(2,1)} %bitcast.184) | data formatting | bytes 4194304 | tf_op jit(solution)/shard_map/reshape | solution.py:188
  18.6 7.9 %all-to-all-start = ((bf16[2,16,128,256]{3,2,0,1:T(8,128)(2,1)}), bf16[2,16,128,256]{3,2,0,1:T(8,128)(2,1)S(1)}, u32[]{:S(2)}, u32[]{:S(2)}) async-start(bf16[2,16,128,256]{3,2,0,1:T(8,128)(2,1)} %copy.81), calls=%async_computation | async-start | bytes 4194304 | tf_op jit(solution)/shard_map/all_to_all | solution.py:191
  26.6 0.5 all-gather.11.cloned.1.call-update
  27.2 41.9 %all_gather.17 = bf16[64,2,16,128]{3,2,1,0:T(8,128)(2,1)S(1)} all-gather(bf16[4,2,16,128]{3,2,1,0:T(8,128)(2,1)} %param.23), channel_id=1, replica_groups=mesh['req'=16,'tensor'=8] {'req'}, dimensions={0}, use_global_device_ids=true | all-gather | bytes 557056 | tf_op jit(solution)/shard_map/all_gather | solution.py:121
  70.2 0.6 slice_bitcast_fusion.4
  70.8 0.7 broadcast_bitcast_fusion
  71.5 7.2 %collective-permute-start.2 = (bf16[512,896]{1,0:T(8,128)(2,1)}, bf16[512,896]{1,0:T(8,128)(2,1)}, u32[]{:S(2)}, u32[]{:S(2)}) collective-permute-start(bf16[512,896]{1,0:T(8,128)(2,1)} %collective-permute-done), channel_id=1, source_target_pairs={{0,1},{1,2},{2,3},{3,4},{4,5},{5,6},{6,7},{7,0},{8,9},{9,10},{10,1... | collective-permute-start | bytes 2752520 | tf_op jit(solution)/shard_map/ppermute | solution.py:90
  78.7 0.7 iota_compare_fusion.2
  79.5 0.8 broadcast_and_fusion
  80.2 3.8 %broadcast_in_dim.46 = bf16[512,7168]{1,0:T(8,128)(2,1)} broadcast(bf16[]{:T(256)} %constant.85.clone.1), dimensions={} | broadcast | bytes 7340034 | tf_op jit(solution)/shard_map/broadcast_in_dim | solution.py:84
  84.1 1.1 constant_dynamic-update-slice_fusion.7
  85.2 1.2 dynamic_slice.10
  86.4 2.9 %collective-permute-done.2 = bf16[512,896]{1,0:T(8,128)(2,1)} collective-permute-done((bf16[512,896]{1,0:T(8,128)(2,1)}, bf16[512,896]{1,0:T(8,128)(2,1)}, u32[]{:S(2)}, u32[]{:S(2)}) %collective-permute-start.2) | collective-permute-done | bytes 917536 | tf_op jit(solution)/shard_map/ppermute | solution.py:90
  89.3 2.5 collective-permute-start.4
  91.8 1.0 multiply_cosine_fusion
  92.8 0.8 fusion.69
  93.7 2.2 constant_dynamic-update-slice_fusion.6
  95.9 6.6 %collective-permute-done.4 = bf16[512,896]{1,0:T(8,128)(2,1)S(1)} collective-permute-done((bf16[512,896]{1,0:T(8,128)(2,1)}, bf16[512,896]{1,0:T(8,128)(2,1)S(1)}, u32[]{:S(2)}, u32[]{:S(2)}) %collective-permute-start.4) | collective-permute-done | bytes 917536 | tf_op jit(solution)/shard_map/ppermute | solution.py:90
  102.4 2.4 collective-permute-start.6
  104.8 2.2 constant_dynamic-update-slice_fusion.5
  107.0 2.2 constant_dynamic-update-slice_fusion.4
  109.3 2.2 constant_dynamic-update-slice_fusion.3
  111.5 1.5 copy.82
  113.0 2.5 convolution_convert_fusion.2
  115.5 1.1 constant_dynamic-update-slice_fusion.2
  116.6 2.2 constant_dynamic-update-slice_fusion.1
  118.8 2.3 constant_dynamic-update-slice_fusion
  121.1 4.7 %fusion = f32[512]{0:T(512)S(1)} fusion(bf16[512,7168]{1,0:T(8,128)(2,1)} %constant_dynamic-update-slice_fusion), kind=kLoop, calls=%fused_computation.3 | loop fusion | flops 11009536 | bytes 7342080 | tf_op jit(solution)/shard_map/reduce_sum | solution.py:104
  125.9 5.8 %fusion.2 = bf16[512,7168]{1,0:T(8,128)(2,1)S(1)} fusion(bf16[512,7168]{1,0:T(8,128)(2,1)} %constant_dynamic-update-slice_fusion, f32[7168]{0:T(1024)S(1)} %copy-done.7, f32[512]{0:T(512)S(1)} %add_rsqrt_fusion), kind=kLoop, calls=%fused_computation.5 | loop fusion | flops 14680064 | bytes 14710784 | tf_op jit(solution)/shard_map/convert_element_type | solution.py:105
  131.8 6.7 %fusion.101 = f32[512,256]{1,0:T(8,128)S(1)} fusion(bf16[512,7168]{1,0:T(8,128)(2,1)S(1)} %fusion.2, bf16[7168,256]{1,0:T(8,128)(2,1)} %param.19), kind=kOutput, calls=%fused_computation.148 | convolution fusion | flops 1879048192 | bytes 11534336 | tf_op jit(solution)/shard_map/dot_general | solution.py:158
  138.7 10.3 %fusion.100 = f32[512,512]{1,0:T(8,128)} fusion(bf16[512,7168]{1,0:T(8,128)(2,1)} %copy-done.2, bf16[7168,512]{1,0:T(8,128)(2,1)} %param.18), kind=kOutput, calls=%fused_computation.147 | convolution fusion | flops 3758096384 | bytes 15728640 | tf_op jit(solution)/shard_map/dot_general | solution.py:149
  149.0 3.8 %fusion.24 = bf16[4,48,896]{2,0,1:T(4,128)(2,1)S(1)} fusion(s32[4]{0:T(128)S(1)} %copy-done.9, bf16[8,8,48,896]{3,2,1,0:T(8,128)(2,1)} %bitcast.201), kind=kOutput, calls=%fused_computation.32 | convolution fusion | flops 22192384 | bytes 5849104 | tf_op jit(solution)/shard_map/dot_general | solution.py:130
  152.8 0.5 convolution_convert_fusion.3
  153.2 23.4 %psum.14 = bf16[4,128,48]{1,2,0:T(8,128)(2,1)S(1)} all-reduce(bf16[4,128,48]{1,2,0:T(8,128)(2,1)S(1)} %convolution_convert_fusion.3), channel_id=1, replica_groups=mesh['req'=16,'tensor'=8] {'tensor'}, use_global_device_ids=true, to_apply=%region_1.2 | all-reduce | flops 24576 | bytes 98304 | tf_op jit(solution)/shard_map/psum | solution.py:144
  176.6 0.3 convolution_multiply_fusion.3
  177.0 1.4 add.206
  178.4 0.4 reshape.494
  178.8 0.6 fusion.98
  180.0 2.8 %fusion.3 = (f32[2,128,4]{1,2,0:T(4,128)S(1)}, f32[2,128,4,2048]{3,1,2,0:T(8,128)S(1)}) fusion(pred[2,2048]{1,0:T(4,128)(4,1)S(1)} %fusion.69, bf16[2,2048,1,256]{3,1,0,2:T(8,128)(2,1)} %bitcast.185, bf16[4,128,1,4,128]{4,1,3,0,2:T(8,128)(2,1)S(1)} %pad_maximum_fusion), kind=kOutput, calls=%fused_computation.9 | convolution fusion | flops 543161344 | bytes 9711616 | tf_op jit(solution)/shard_map/bsvgd,bkvd->bvsgk/dot_general | solution.py:30
  182.9 2.2 fusion.4
  185.1 2.3 fusion.21
  187.7 0.6 fusion.68
  188.3 0.5 fusion.99
  189.0 1.1 bitcast_multiply_fusion
  190.2 1.8 fusion.20
  192.0 0.3 copy.86
  192.3 9.2 %convolution_convert_fusion = bf16[512,7168]{1,0:T(8,128)(2,1)} fusion(bf16[512,7168]{1,0:T(8,128)(2,1)} %param.20, bf16[64,8,4,128]{3,2,1,0:T(4,128)(2,1)S(1)} %bitcast.195), kind=kOutput, calls=%fused_computation.6 | convolution fusion | flops 3761766400 | bytes 15204352 | tf_op jit(solution)/shard_map/dot_general | solution.py:223
  201.5 10.4 %copy.105 = bf16[512,7168]{0,1:T(8,128)(2,1)} copy(bf16[512,7168]{1,0:T(8,128)(2,1)} %convolution_convert_fusion) | data formatting | bytes 14680064
  212.0 0.6 copy-done.10
  212.6 2.5 convolution_convert_fusion.1
  215.1 5.5 %all-gather.11.cloned.1.call-done = bf16[64,16,896]{2,1,0:T(8,128)(2,1)} async-done(((bf16[4,16,896]{2,1,0:T(8,128)(2,1)}), bf16[64,16,896]{2,1,0:T(8,128)(2,1)}) %all-gather.11.cloned.1.call-update) | async-done | bytes 1835024 | tf_op jit(solution)/shard_map/all_gather | solution.py:123
  220.6 2.0 fusion.28
  222.7 22.9 %psum.15 = bf16[4,128,16]{1,2,0:T(8,128)(2,1)S(1)} all-reduce(bf16[4,128,16]{1,2,0:T(8,128)(2,1)S(1)} %convolution_convert_fusion.5), channel_id=1, replica_groups=mesh['req'=16,'tensor'=8] {'tensor'}, use_global_device_ids=true, to_apply=%region_7.8 | all-reduce | flops 8192 | bytes 32768 | tf_op jit(solution)/shard_map/psum | solution.py:231
  245.6 1.7 convolution_multiply_fusion
  247.4 23.2 %reduce-scatter.4.cloned.1.call-done = bf16[896,512]{1,0:T(8,128)(2,1)} async-done(((bf16[7168,512]{1,0:T(8,128)(2,1)}), bf16[896,512]{1,0:T(8,128)(2,1)}) %reduce-scatter.4.cloned.1.call-update) | async-done | bytes 917520
  270.5 1.5 copy.106
  272.1 2.6 fusion.15
  (78 shorter events, 3.4 us)
Async XLA Ops:
  6.5 6.9 %copy-start = (bf16[32,128,256]{2,1,0:T(8,128)(2,1)S(1)}, bf16[32,128,256]{2,1,0:T(8,128)(2,1)}, u32[]{:S(2)}) copy-start(bf16[32,128,256]{2,1,0:T(8,128)(2,1)} %param.31) | copy-start | bytes 6291460
  6.5 62.6 %copy-start.14 = (s32[32]{0:T(128)S(1)}, s32[32]{0:T(128)}, u32[]{:S(2)}) copy-start(s32[32]{0:T(128)} %param.28) | copy-start | bytes 388
  6.5 106.5 %all-gather.7.cloned.1.call-start = ((), (), s32[]{:S(2)}) async-start(), calls=%async_computation.3 | async-start | bytes 1114112 | tf_op jit(solution)/shard_map/all_gather | solution.py:120
  7.3 141.7 %all-gather.5.cloned.1.call-start = ((), (), s32[]{:S(2)}) async-start(), calls=%async_computation.2 | async-start | bytes 5849088 | tf_op jit(solution)/shard_map/all_gather | solution.py:119
  8.0 204.0 %all-gather.9.cloned.1.call-start = ((), (), s32[]{:S(2)}) async-start(), calls=%async_computation.4 | async-start | bytes 1114112 | tf_op jit(solution)/shard_map/all_gather | solution.py:122
  8.7 62.7 %collective-permute-start = (bf16[512,896]{1,0:T(8,128)(2,1)}, bf16[512,896]{1,0:T(8,128)(2,1)}, u32[]{:S(2)}, u32[]{:S(2)}) collective-permute-start(bf16[512,896]{1,0:T(8,128)(2,1)} %param.16), channel_id=1, source_target_pairs={{0,1},{1,2},{2,3},{3,4},{4,5},{5,6},{6,7},{7,0},{8,9},{9,10},{10,1... | collective-permute-start | bytes 2752520 | tf_op jit(solution)/shard_map/ppermute | solution.py:90
  11.3 68.9 %collective-permute-start.1 = (bf16[512,896]{1,0:T(8,128)(2,1)}, bf16[512,896]{1,0:T(8,128)(2,1)}, u32[]{:S(2)}, u32[]{:S(2)}) collective-permute-start(bf16[512,896]{1,0:T(8,128)(2,1)} %param.16), channel_id=1, source_target_pairs={{0,7},{1,0},{2,1},{3,2},{4,3},{5,4},{6,5},{7,6},{8,15},{9,8},{10,9... | collective-permute-start | bytes 2752520 | tf_op jit(solution)/shard_map/ppermute | solution.py:96
  13.5 56.3 %copy-start.13 = (s32[32]{0:T(128)S(1)}, s32[32]{0:T(128)}, u32[]{:S(2)}) copy-start(s32[32]{0:T(128)} %param.29) | copy-start | bytes 388
  13.5 56.4 %copy-start.8 = (s32[4]{0:T(128)S(1)}, s32[4]{0:T(128)}, u32[]{:S(2)}) copy-start(s32[4]{0:T(128)} %param.26) | copy-start | bytes 52
  18.6 65.4 %copy-start.4 = (bf16[512,896]{1,0:T(8,128)(2,1)S(1)}, bf16[512,896]{1,0:T(8,128)(2,1)}, u32[]{:S(2)}) copy-start(bf16[512,896]{1,0:T(8,128)(2,1)} %param.16) | copy-start | bytes 2752516
  18.6 92.8 %all-to-all-start = ((bf16[2,16,128,256]{3,2,0,1:T(8,128)(2,1)}), bf16[2,16,128,256]{3,2,0,1:T(8,128)(2,1)S(1)}, u32[]{:S(2)}, u32[]{:S(2)}) async-start(bf16[2,16,128,256]{3,2,0,1:T(8,128)(2,1)} %copy.81), calls=%async_computation | async-start | bytes 4194304 | tf_op jit(solution)/shard_map/all_to_all | solution.py:191
  26.5 194.1 %all-gather.11.cloned.1.call-start = ((), (), s32[]{:S(2)}) async-start(), calls=%async_computation.5 | async-start | bytes 1949696 | tf_op jit(solution)/shard_map/all_gather | solution.py:123
  27.1 243.4 %reduce-scatter.4.cloned.1.call-start = ((), (), s32[]{:S(2)}) async-start(), calls=%async_computation.6 | async-start | bytes 8257536
  71.5 17.8 %collective-permute-start.2 = (bf16[512,896]{1,0:T(8,128)(2,1)}, bf16[512,896]{1,0:T(8,128)(2,1)}, u32[]{:S(2)}, u32[]{:S(2)}) collective-permute-start(bf16[512,896]{1,0:T(8,128)(2,1)} %collective-permute-done), channel_id=1, source_target_pairs={{0,1},{1,2},{2,3},{3,4},{4,5},{5,6},{6,7},{7,0},{8,9},{9,10},{10,1... | collective-permute-start | bytes 2752520 | tf_op jit(solution)/shard_map/ppermute | solution.py:90
  79.4 12.3 %copy-start.11 = (pred[4,128]{1,0:T(4,128)(4,1)}, pred[4,128]{1,0:T(4,128)(4,1)S(1)}, u32[]{:S(2)}) copy-start(pred[4,128]{1,0:T(4,128)(4,1)S(1)} %iota_compare_fusion.2) | copy-start | bytes 1540
  80.2 13.4 %collective-permute-start.3 = (bf16[512,896]{1,0:T(8,128)(2,1)}, bf16[512,896]{1,0:T(8,128)(2,1)}, u32[]{:S(2)}, u32[]{:S(2)}) collective-permute-start(bf16[512,896]{1,0:T(8,128)(2,1)} %collective-permute-done.1), channel_id=1, source_target_pairs={{0,7},{1,0},{2,1},{3,2},{4,3},{5,4},{6,5},{7,6},{8,15},{9,8},{10,9... | collective-permute-start | bytes 2752520 | tf_op jit(solution)/shard_map/ppermute | solution.py:96
  89.3 13.1 %collective-permute-start.4 = (bf16[512,896]{1,0:T(8,128)(2,1)}, bf16[512,896]{1,0:T(8,128)(2,1)S(1)}, u32[]{:S(2)}, u32[]{:S(2)}) collective-permute-start(bf16[512,896]{1,0:T(8,128)(2,1)} %collective-permute-done.2), channel_id=1, source_target_pairs={{0,1},{1,2},{2,3},{3,4},{4,5},{5,6},{6,7},{7,0},{8,9},{9,10},{10,1... | collective-permute-start | bytes 2752520 | tf_op jit(solution)/shard_map/ppermute | solution.py:90
  93.7 22.9 %collective-permute-start.5 = (bf16[512,896]{1,0:T(8,128)(2,1)}, bf16[512,896]{1,0:T(8,128)(2,1)}, u32[]{:S(2)}, u32[]{:S(2)}) collective-permute-start(bf16[512,896]{1,0:T(8,128)(2,1)} %collective-permute-done.3), channel_id=1, source_target_pairs={{0,7},{1,0},{2,1},{3,2},{4,3},{5,4},{6,5},{7,6},{8,15},{9,8},{10,9... | collective-permute-start | bytes 2752520 | tf_op jit(solution)/shard_map/ppermute | solution.py:96
  102.4 16.4 %collective-permute-start.6 = (bf16[512,896]{1,0:T(8,128)(2,1)S(1)}, bf16[512,896]{1,0:T(8,128)(2,1)}, u32[]{:S(2)}, u32[]{:S(2)}) collective-permute-start(bf16[512,896]{1,0:T(8,128)(2,1)S(1)} %collective-permute-done.4), channel_id=1, source_target_pairs={{0,1},{1,2},{2,3},{3,4},{4,5},{5,6},{6,7},{7,0},{8,9},{9,10},{10,1... | collective-permute-start | bytes 2752520 | tf_op jit(solution)/shard_map/ppermute | solution.py:90
  113.0 12.9 %copy-start.7 = (f32[7168]{0:T(1024)S(1)}, f32[7168]{0:T(1024)}, u32[]{:S(2)}) copy-start(f32[7168]{0:T(1024)} %param.17) | copy-start | bytes 86020
  131.7 6.8 %copy-start.2 = (bf16[512,7168]{1,0:T(8,128)(2,1)}, bf16[512,7168]{1,0:T(8,128)(2,1)S(1)}, u32[]{:S(2)}) copy-start(bf16[512,7168]{1,0:T(8,128)(2,1)S(1)} %fusion.2) | copy-start | bytes 22020100
  138.6 10.3 %copy-start.9 = (s32[4]{0:T(128)S(1)}, s32[4]{0:T(128)}, u32[]{:S(2)}) copy-start(s32[4]{0:T(128)} %param.26) | copy-start | bytes 52
  180.0 5.1 %copy-start.3 = (bf16[2,16,128,256]{3,2,1,0:T(8,128)(2,1)S(1)}, bf16[2,16,128,256]{3,2,1,0:T(8,128)(2,1)}, u32[]{:S(2)}) copy-start(bf16[2,16,128,256]{3,2,1,0:T(8,128)(2,1)} %copy.82) | copy-start | bytes 6291460
  185.1 2.4 copy-start.6
  185.1 3.2 %copy-start.5 = (pred[4,128,128]{1,2,0:T(8,128)(4,1)S(1)}, pred[4,128,128]{1,2,0:T(8,128)(4,1)}, u32[]{:S(2)}) copy-start(pred[4,128,128]{1,2,0:T(8,128)(4,1)} %broadcast_and_fusion) | copy-start | bytes 196612
  187.4 2.8 copy-start.12
  211.9 0.7 copy-start.10
  212.0 62.7 %copy-start.1 = (bf16[32,128,256]{2,1,0:T(8,128)(2,1)S(1)}, bf16[32,128,256]{2,1,0:T(8,128)(2,1)}, u32[]{:S(2)}) copy-start(bf16[32,128,256]{2,1,0:T(8,128)(2,1)} %param.31) | copy-start | bytes 6291460
Sparse Core Ops, SparseCore 0:
  9.5 61.2 all-gather.6
  72.9 58.6 all-gather.4
  133.7 40.6 all-gather.8
  176.4 44.1 all-gather.10
  222.9 47.6 reduce-scatter.3
